TPU v7x, 256 devices: a whole 4x4x8 slice. The times are simulated.
256 devices in a mesh: pb: 8 (over y, core), kv: 32 (over z, x).
Axes of the slice: x: 4, y: 4, z: 8, core: 2. Of those that a mesh axis runs over, the one named last changes fastest.
Arguments:
- queries: bfloat16 [65536, 4096], P(('pb', 'kv')), may hold values from -6 to 6
- keys: bfloat16 [8192, 4096], P(('pb', 'kv')), may hold values from -6 to 6
- values: bfloat16 [8192, 4096], P(('pb', 'kv')), may hold values from -6 to 6
- key_lists: int32 [512, 8], P('pb'), may hold values from 0 to 63, as said below
- counts: int32 [512], P('pb'), may hold values from 1 to 8, as said below
Outputs:
- attended: bfloat16 [65536, 4096], P(('pb', 'kv'))
Inputs may be any that keep to these rules, and one draw needn't show every extreme that they name: For every query block the first counts entries of its row of key_lists name different key blocks; entries past counts are valid block numbers that do not take part. `counts`: some query block uses all 8 entries of its list.
All inputs are finite; a program needn't handle non-finite values.
Results may differ from a plain program's by a relative error of at most 0.011.
Values may be sent and summed in bfloat16 or wider, within the bound.
No kernel may reach another device: no remote copies, remote signals or barrier semaphores. Data moves between devices by JAX's collectives and lax.ppermute only.
A program may use at most 64 MiB of HBM per device.

v0:
```python
import math
import jax
import jax.numpy as jnp
from jax import lax
from jax.sharding import PartitionSpec as P

HEADS = 32
HD = 128
BLK = 128
MOST = 8


def regroup(split_array, kv_count, pb_count):
    tokens_each = split_array.shape[0] // (kv_count * pb_count)
    shaped = split_array.reshape(kv_count, pb_count, tokens_each, split_array.shape[1])
    return shaped.transpose(1, 0, 2, 3).reshape(-1, split_array.shape[1])


def per_device(queries, keys, values, key_lists, counts):
    kv_count = lax.axis_size("kv")
    pb_count = lax.axis_size("pb")
    head_local = HEADS // kv_count
    scaling = HD ** (-0.5)
    key_whole, value_whole = (
        lax.all_gather(keys, "pb", axis=0, tiled=True),
        lax.all_gather(values, "pb", axis=0, tiled=True),
    )
    key_split, value_split = (
        lax.all_to_all(key_whole, "kv", split_axis=1, concat_axis=0, tiled=True),
        lax.all_to_all(value_whole, "kv", split_axis=1, concat_axis=0, tiled=True),
    )
    key_heads = regroup(key_split, kv_count, pb_count)
    value_heads = regroup(value_split, kv_count, pb_count)
    key_blocks = key_heads.reshape(-1, BLK, head_local, HD)
    value_blocks = value_heads.reshape(-1, BLK, head_local, HD)
    slot_of_key = jnp.arange(MOST * BLK, dtype=jnp.int32) // BLK

    def padded_group(item):
        group_queries, group_lists, group_counts = item
        members = group_queries.shape[0]
        listed_keys = key_blocks[group_lists].reshape(members, MOST * BLK, head_local, HD)
        listed_values = value_blocks[group_lists].reshape(members, MOST * BLK, head_local, HD)
        scores = (
            jnp.einsum(
                "gqhd,gkhd->ghqk", group_queries, listed_keys, preferred_element_type=jnp.float32
            )
            * scaling
        )
        usable = (slot_of_key[None, :] < group_counts[:, None])[:, None, None, :]
        largest = jnp.max(jnp.where(usable, scores, -jnp.inf), axis=-1, keepdims=True)
        raised = jnp.where(usable, jnp.exp(scores - largest), 0.0)
        totals = jnp.sum(raised, axis=-1, keepdims=True)
        weights = (raised / totals).astype(jnp.bfloat16)
        output = jnp.einsum(
            "ghqk,gkhd->gqhd", weights, listed_values, preferred_element_type=jnp.float32
        )
        return output.astype(jnp.bfloat16)

    query_blocks = queries.reshape(-1, BLK, queries.shape[1])
    exchanged = lax.all_to_all(query_blocks, "kv", split_axis=2, concat_axis=0, tiled=True)
    block_total = exchanged.shape[0]
    rows = exchanged.shape[1]
    per_group = math.gcd(block_total, max(1, 512 // rows))
    group_total = block_total // per_group
    grouped = exchanged.reshape(group_total, per_group, rows, head_local, HD)
    lists_grouped = key_lists.reshape(group_total, per_group, key_lists.shape[1])
    counts_grouped = counts.reshape(group_total, per_group)
    produced = lax.map(padded_group, (grouped, lists_grouped, counts_grouped))
    joined = produced.reshape(block_total, rows, head_local * HD)
    result = lax.all_to_all(joined, "kv", split_axis=0, concat_axis=2, tiled=True)
    return result.reshape(queries.shape)


def solution(mesh):
    return jax.shard_map(
        per_device,
        mesh=mesh,
        in_specs=(
            P(("pb", "kv"), None),
            P(("pb", "kv"), None),
            P(("pb", "kv"), None),
            P("pb", None),
            P("pb"),
        ),
        out_specs=P(("pb", "kv"), None),
        check_vma=False,
    )
```

profile of v0, /device:TPU:2, one launch (start us, length us, event | category | flops | bytes accessed | tf_op | source)
XLA Modules:
  0.0 411.0 jit_solution(12888155072686574849)
XLA Ops:
  6.5 6.2 %copy.31 = bf16[2,128,4096]{1,0,2:T(2,128)(2,1)} copy(bf16[2,128,4096]{2,1,0:T(8,128)(2,1)} %bitcast.84) | data formatting | bytes 4194304 | tf_op jit(solution)/shard_map/reshape | solution.py:59
  12.7 11.6 %all-to-all-start.1 = ((bf16[2,128,4096]{1,0,2:T(2,128)(2,1)}), bf16[2,128,4096]{1,0,2:T(2,128)(2,1)S(1)}, u32[]{:S(2)}, u32[]{:S(2)}) async-start(bf16[2,128,4096]{1,0,2:T(2,128)(2,1)} %copy.31), calls=%async_computation.1 | async-start | bytes 4194304 | tf_op jit(solution)/shard_map/all_to_all | solution.py:60
  25.1 30.8 %all-gather.5.cloned.1.call-done = bf16[256,4096]{1,0:T(8,128)(2,1)} async-done(((bf16[32,4096]{1,0:T(8,128)(2,1)}), bf16[256,4096]{1,0:T(8,128)(2,1)}) %all-gather.5.cloned.1.call-update) | async-done | bytes 2097168 | tf_op jit(solution)/shard_map/all_gather | solution.py:25
  55.9 4.1 copy.34
  60.0 13.6 %all-to-all-done.1 = bf16[2,128,4096]{1,0,2:T(2,128)(2,1)S(1)} async-done(((bf16[2,128,4096]{1,0,2:T(2,128)(2,1)}), bf16[2,128,4096]{1,0,2:T(2,128)(2,1)S(1)}, u32[]{:S(2)}, u32[]{:S(2)}) %all-to-all-start.1) | async-done | bytes 2097184 | tf_op jit(solution)/shard_map/all_to_all | solution.py:60
  73.6 6.9 %all-to-all-start.2 = ((bf16[256,32,128]{0,2,1:T(8,128)(2,1)}), bf16[256,32,128]{0,2,1:T(8,128)(2,1)}, u32[]{:S(2)}, u32[]{:S(2)}) async-start(bf16[256,32,128]{0,2,1:T(8,128)(2,1)} %bitcast.76), calls=%async_computation.2 | async-start | bytes 4194304 | tf_op jit(solution)/shard_map/all_to_all | solution.py:29
  81.2 30.8 %all-gather.3.cloned.1.call-done = bf16[256,4096]{1,0:T(8,128)(2,1)} async-done(((bf16[32,4096]{1,0:T(8,128)(2,1)}), bf16[256,4096]{1,0:T(8,128)(2,1)}) %all-gather.3.cloned.1.call-update) | async-done | bytes 2097168 | tf_op jit(solution)/shard_map/all_gather | solution.py:26
  112.1 4.1 copy.28
  116.1 12.9 %all-to-all-done.2 = bf16[256,32,128]{0,2,1:T(8,128)(2,1)} async-done(((bf16[256,32,128]{0,2,1:T(8,128)(2,1)}), bf16[256,32,128]{0,2,1:T(8,128)(2,1)}, u32[]{:S(2)}, u32[]{:S(2)}) %all-to-all-start.2) | async-done | bytes 2097184 | tf_op jit(solution)/shard_map/all_to_all | solution.py:29
  129.1 6.7 %all-to-all-start = ((bf16[256,32,128]{0,2,1:T(8,128)(2,1)}), bf16[256,32,128]{0,2,1:T(8,128)(2,1)}, u32[]{:S(2)}, u32[]{:S(2)}) async-start(bf16[256,32,128]{0,2,1:T(8,128)(2,1)} %bitcast.77), calls=%async_computation | async-start | bytes 4194304 | tf_op jit(solution)/shard_map/all_to_all | solution.py:30
  137.7 4.1 copy.33
  141.7 4.1 copy.35
  147.8 37.0 %all-to-all-done = bf16[256,32,128]{0,2,1:T(8,128)(2,1)} async-done(((bf16[256,32,128]{0,2,1:T(8,128)(2,1)}), bf16[256,32,128]{0,2,1:T(8,128)(2,1)}, u32[]{:S(2)}, u32[]{:S(2)}) %all-to-all-start) | async-done | bytes 2097184 | tf_op jit(solution)/shard_map/all_to_all | solution.py:30
  184.8 4.1 copy.29
  188.9 3.4 copy.30
  192.2 154.8 %while.11 = (s32[]{:T(128)}, bf16[16,4,128,1,128]{4,2,1,0,3:T(8,128)(2,1)}, s32[16,4,8]{2,1,0:T(4,128)S(1)}, bf16[64,128,1,128]{3,1,0,2:T(8,128)(2,1)}, s32[16,4...) while((s32[]{:T(128)}, ...), condition=%wide.region_3.4_spmd.clone, body=%wide.region_0.3_spmd.clone.sunk | while | flops 272709728 | bytes 15493133 | solution.py:68
  196.5 2.3 gather_fusion
  198.9 2.2 fusion.37
  206.2 2.3 gather_fusion
  208.6 2.2 fusion.37
  215.9 2.3 gather_fusion
  218.2 2.2 fusion.37
  225.6 2.3 gather_fusion
  227.9 2.2 fusion.37
  235.2 2.3 gather_fusion
  237.6 2.2 fusion.37
  244.9 2.3 gather_fusion
  247.3 2.2 fusion.37
  254.6 2.3 gather_fusion
  264.3 2.3 gather_fusion
  266.6 2.2 fusion.37
  273.9 2.3 gather_fusion
  276.3 2.2 fusion.37
  283.6 2.3 gather_fusion
  285.9 2.2 fusion.37
  293.3 2.3 gather_fusion
  295.6 2.2 fusion.37
  302.9 2.3 gather_fusion
  305.3 2.2 fusion.37
  312.6 2.3 gather_fusion
  315.0 2.2 fusion.37
  322.3 2.3 gather_fusion
  324.6 2.2 fusion.37
  332.0 2.3 gather_fusion
  341.6 2.3 gather_fusion
  344.0 2.2 fusion.37
  347.0 53.5 %all_to_all.62 = bf16[64,128,128]{2,1,0:T(8,128)(2,1)S(1)} all-to-all(bf16[64,128,128]{2,1,0:T(8,128)(2,1)} %bitcast.85), channel_id=1, replica_groups=mesh['pb'=8,'kv'=32] {'kv'}, dimensions={0} | all-to-all | bytes 4194304 | tf_op jit(solution)/shard_map/all_to_all | solution.py:70
  401.8 2.3 copy.45
  (192 shorter events, 92.5 us)
Async XLA Ops:
  12.7 60.9 %all-to-all-start.1 = ((bf16[2,128,4096]{1,0,2:T(2,128)(2,1)}), bf16[2,128,4096]{1,0,2:T(2,128)(2,1)S(1)}, u32[]{:S(2)}, u32[]{:S(2)}) async-start(bf16[2,128,4096]{1,0,2:T(2,128)(2,1)} %copy.31), calls=%async_computation.1 | async-start | bytes 4194304 | tf_op jit(solution)/shard_map/all_to_all | solution.py:60
  24.3 31.6 %all-gather.5.cloned.1.call-start = ((), (), s32[]{:S(2)}) async-start(), calls=%async_computation.5 | async-start | bytes 2359296 | tf_op jit(solution)/shard_map/all_gather | solution.py:25
  73.6 55.5 %all-to-all-start.2 = ((bf16[256,32,128]{0,2,1:T(8,128)(2,1)}), bf16[256,32,128]{0,2,1:T(8,128)(2,1)}, u32[]{:S(2)}, u32[]{:S(2)}) async-start(bf16[256,32,128]{0,2,1:T(8,128)(2,1)} %bitcast.76), calls=%async_computation.2 | async-start | bytes 4194304 | tf_op jit(solution)/shard_map/all_to_all | solution.py:29
  80.5 31.6 %all-gather.3.cloned.1.call-start = ((), (), s32[]{:S(2)}) async-start(), calls=%async_computation.4 | async-start | bytes 2359296 | tf_op jit(solution)/shard_map/all_gather | solution.py:26
  129.1 6.8 %copy-start = (s32[64,8]{0,1:T(8,128)S(1)}, s32[64,8]{0,1:T(8,128)}, u32[]{:S(2)}) copy-start(s32[64,8]{0,1:T(8,128)} %param.10) | copy-start | bytes 6148
  129.1 6.9 %copy-start.1 = (s32[64]{0:T(128)S(1)}, s32[64]{0:T(128)}, u32[]{:S(2)}) copy-start(s32[64]{0:T(128)} %param.11) | copy-start | bytes 772
  129.1 55.7 %all-to-all-start = ((bf16[256,32,128]{0,2,1:T(8,128)(2,1)}), bf16[256,32,128]{0,2,1:T(8,128)(2,1)}, u32[]{:S(2)}, u32[]{:S(2)}) async-start(bf16[256,32,128]{0,2,1:T(8,128)(2,1)} %bitcast.77), calls=%async_computation | async-start | bytes 4194304 | tf_op jit(solution)/shard_map/all_to_all | solution.py:30
Sparse Core Ops, SparseCore 0:
  27.0 28.8 all-gather.4
  83.2 28.8 all-gather.2
where the time goes:
time: 413 us; the launch traced here: 411 us
  waiting for transfers between devices  127 us (31%)
  local copies, waits for them, and re-layouts  101 us (24%)
  matrix products  56.6 us (14%)
  blocking collectives  53.5 us (13%)
  other arithmetic  33.6 us (8%)
  starting transfers between devices  25.4 us (6%)
  between operations  13.5 us (3%)
    all_to_all x1, blocking collectives, per_device(): lax.all_to_all(joined, 'kv', split_axis=0, concat_axis=2, tiled=True)  53.5 us
    gather x16, local copies, waits for them, and re-layouts, padded_group(): value_blocks[group_lists].reshape(members, MOST * BLK, head_local, HD)  37.4 us
    all_to_all x1, waiting for transfers between devices, per_device(): lax.all_to_all(value_whole, 'kv', split_axis=1, concat_axis=0, tiled=True)  37 us
    dot_general x16, matrix products, padded_group(): jnp.einsum('ghqk,gkhd->gqhd', weights, listed_values, preferred_element_t...  35.1 us
    sub x16, other arithmetic, padded_group(): raised = jnp.where(usable, jnp.exp(scores - largest), 0.0)  32.1 us
    all_gather x1, waiting for transfers between devices, per_device(): lax.all_gather(keys, 'pb', axis=0, tiled=True)  30.8 us
    all_gather x1, waiting for transfers between devices, per_device(): lax.all_gather(values, 'pb', axis=0, tiled=True)  30.8 us
    dot_general x16, matrix products, padded_group(): jnp.einsum('gqhd,gkhd->ghqk', group_queries, listed_keys, preferred_eleme...  21.5 us
  transfers between devices with their start and end apart: 5, of which 5 were waited for; matrix products, arithmetic and copies ran while one was open for 5% of the time, Pallas kernels for 0%

commit v1 on v0

--- a/solution.py
+++ b/solution.py
@@ -26,7 +26,12 @@
         lax.all_gather(values, "pb", axis=0, tiled=True),
     )
     key_split, value_split = (
-        lax.all_to_all(key_whole, "kv", split_axis=1, concat_axis=0, tiled=True),
+        jnp.concatenate(
+            lax.all_to_all(
+                jnp.stack(jnp.split(key_whole, lax.axis_size("kv"), axis=1)), "kv", 0, 0
+            ),
+            axis=0,
+        ),
         lax.all_to_all(value_whole, "kv", split_axis=1, concat_axis=0, tiled=True),
     )
     key_heads = regroup(key_split, kv_count, pb_count)

time: 413 us -> 435 us (1.053)
  local copies, waits for them, and re-layouts: 101 us -> 140 us
  waiting for transfers between devices: 127 us -> 103 us
    unnamed x6 -> x37, local copies, waits for them, and re-layouts: 2.39 us -> 47.9 us
    all_gather x1, waiting for transfers between devices: 30.8 us -> 14.9 us  [per_device(): lax.all_gather(keys, 'pb', axis=0, tiled=True)]
    all_to_all x1, waiting for transfers between devices: 13.6 us -> 0.01 us  [per_device(): lax.all_to_all(query_blocks, 'kv', split_axis=2, concat_axis=0, tiled=True)]
    all_to_all x1, waiting for transfers between devices: 37 us -> 41.4 us  [per_device(): lax.all_to_all(value_whole, 'kv', split_axis=1, concat_axis=0, tiled=True)]
  transfers between devices with their start and end apart: 5 -> 5, of which waited for: 5 -> 4; matrix products, arithmetic and copies ran while one was open for 5% -> 15% of each run, Pallas kernels for 0% -> 0%
where the time goes in v1:
time: 435 us; the launch traced here: 432 us
  local copies, waits for them, and re-layouts  140 us (32%)
  waiting for transfers between devices  103 us (24%)
  matrix products  56.6 us (13%)
  blocking collectives  56.4 us (13%)
  other arithmetic  33.7 us (8%)
  starting transfers between devices  28.3 us (7%)
  between operations  13.5 us (3%)
    all_to_all x1, blocking collectives, per_device(): lax.all_to_all(joined, 'kv', split_axis=0, concat_axis=2, tiled=True)  56.4 us
    unnamed x37, local copies, waits for them, and re-layouts  47.9 us
    all_to_all x1, waiting for transfers between devices, per_device(): lax.all_to_all(value_whole, 'kv', split_axis=1, concat_axis=0, tiled=True)  41.4 us
    gather x16, local copies, waits for them, and re-layouts, padded_group(): value_blocks[group_lists].reshape(members, MOST * BLK, head_local, HD)  37.4 us
    dot_general x16, matrix products, padded_group(): jnp.einsum('ghqk,gkhd->gqhd', weights, listed_values, preferred_element_t...  35.1 us
    sub x16, other arithmetic, padded_group(): raised = jnp.where(usable, jnp.exp(scores - largest), 0.0)  32.2 us
    all_gather x1, waiting for transfers between devices, per_device(): lax.all_gather(values, 'pb', axis=0, tiled=True)  29.7 us
    dot_general x16, matrix products, padded_group(): jnp.einsum('gqhd,gkhd->ghqk', group_queries, listed_keys, preferred_eleme...  21.4 us
  transfers between devices with their start and end apart: 5, of which 4 were waited for; matrix products, arithmetic and copies ran while one was open for 15% of the time, Pallas kernels for 0%

profile of v1, /device:TPU:2, one launch (start us, length us, event | category | flops | bytes accessed | tf_op | source)
XLA Modules:
  0.0 431.8 jit_solution(7831437858280431170)
XLA Ops:
  7.3 6.2 %copy.29 = bf16[2,128,4096]{1,0,2:T(2,128)(2,1)} copy(bf16[2,128,4096]{2,1,0:T(8,128)(2,1)} %bitcast.208) | data formatting | bytes 4194304 | tf_op jit(solution)/shard_map/reshape | solution.py:64
  13.4 11.6 %all-to-all-start.1 = ((bf16[2,128,4096]{1,0,2:T(2,128)(2,1)}), bf16[2,128,4096]{1,0,2:T(2,128)(2,1)S(1)}, u32[]{:S(2)}, u32[]{:S(2)}) async-start(bf16[2,128,4096]{1,0,2:T(2,128)(2,1)} %copy.29), calls=%async_computation.1 | async-start | bytes 4194304 | tf_op jit(solution)/shard_map/all_to_all | solution.py:65
  25.0 14.9 %all-gather.5.cloned.1.call-done = bf16[256,4096]{1,0:T(8,128)(2,1)} async-done(((bf16[32,4096]{1,0:T(8,128)(2,1)}), bf16[256,4096]{1,0:T(8,128)(2,1)}) %all-gather.5.cloned.1.call-update) | async-done | bytes 2097168 | tf_op jit(solution)/shard_map/all_gather | solution.py:25
  86.9 10.2 %all-to-all-start.2 = ((bf16[32,256,128]{2,1,0:T(8,128)(2,1)}), bf16[32,256,128]{2,1,0:T(8,128)(2,1)}, u32[]{:S(2)}, u32[]{:S(2)}) async-start(bf16[32,256,128]{2,1,0:T(8,128)(2,1)} %constant_dynamic-update-slice_fusion.1), calls=%async_computation.2 | async-start | bytes 4194304 | tf_op jit(solution)/shard_map/all_to_all | solution.py:30
  97.9 29.7 %all-gather.3.cloned.1.call-done = bf16[256,4096]{1,0:T(8,128)(2,1)} async-done(((bf16[32,4096]{1,0:T(8,128)(2,1)}), bf16[256,4096]{1,0:T(8,128)(2,1)}) %all-gather.3.cloned.1.call-update) | async-done | bytes 2097168 | tf_op jit(solution)/shard_map/all_gather | solution.py:26
  127.6 4.1 copy.26
  131.6 15.2 %all-to-all-done.2 = bf16[32,256,128]{2,1,0:T(8,128)(2,1)} async-done(((bf16[32,256,128]{2,1,0:T(8,128)(2,1)}), bf16[32,256,128]{2,1,0:T(8,128)(2,1)}, u32[]{:S(2)}, u32[]{:S(2)}) %all-to-all-start.2) | async-done | bytes 2097184 | tf_op jit(solution)/shard_map/all_to_all | solution.py:30
  146.8 6.5 %all-to-all-start = ((bf16[256,32,128]{0,2,1:T(8,128)(2,1)}), bf16[256,32,128]{0,2,1:T(8,128)(2,1)}, u32[]{:S(2)}, u32[]{:S(2)}) async-start(bf16[256,32,128]{0,2,1:T(8,128)(2,1)} %bitcast.202), calls=%async_computation | async-start | bytes 4194304 | tf_op jit(solution)/shard_map/all_to_all | solution.py:35
  155.2 4.1 copy.31
  159.2 2.0 copy.32
  161.3 41.4 %all-to-all-done = bf16[256,32,128]{0,2,1:T(8,128)(2,1)} async-done(((bf16[256,32,128]{0,2,1:T(8,128)(2,1)}), bf16[256,32,128]{0,2,1:T(8,128)(2,1)}, u32[]{:S(2)}, u32[]{:S(2)}) %all-to-all-start) | async-done | bytes 2097184 | tf_op jit(solution)/shard_map/all_to_all | solution.py:35
  202.7 4.1 copy.27
  206.7 3.4 copy.28
  210.1 154.8 %while.11 = (s32[]{:T(128)}, bf16[16,4,128,1,128]{4,2,1,0,3:T(8,128)(2,1)}, s32[16,4,8]{2,1,0:T(4,128)S(1)}, bf16[64,128,1,128]{3,1,0,2:T(8,128)(2,1)}, s32[16,4...) while((s32[]{:T(128)}, ...), condition=%wide.region_3.4_spmd.clone, body=%wide.region_0.3_spmd.clone.sunk | while | flops 272709728 | bytes 15493133 | solution.py:73
  214.4 2.3 gather_fusion
  216.8 2.2 fusion.37
  224.1 2.3 gather_fusion
  226.4 2.2 fusion.37
  233.8 2.3 gather_fusion
  236.1 2.2 fusion.37
  243.4 2.3 gather_fusion
  245.8 2.2 fusion.37
  253.1 2.3 gather_fusion
  255.5 2.2 fusion.37
  262.8 2.3 gather_fusion
  265.1 2.2 fusion.37
  272.5 2.3 gather_fusion
  274.8 2.2 fusion.37
  282.1 2.3 gather_fusion
  284.5 2.2 fusion.37
  291.8 2.3 gather_fusion
  294.2 2.2 fusion.37
  301.5 2.3 gather_fusion
  303.8 2.2 fusion.37
  311.2 2.3 gather_fusion
  313.5 2.2 fusion.37
  320.8 2.3 gather_fusion
  323.2 2.2 fusion.37
  330.5 2.3 gather_fusion
  332.9 2.2 fusion.37
  340.2 2.3 gather_fusion
  342.5 2.2 fusion.37
  349.9 2.3 gather_fusion
  352.2 2.2 fusion.37
  359.5 2.3 gather_fusion
  361.9 2.2 fusion.37
  364.9 56.4 %all_to_all.51 = bf16[64,128,128]{2,1,0:T(8,128)(2,1)S(1)} all-to-all(bf16[64,128,128]{2,1,0:T(8,128)(2,1)} %bitcast.209), channel_id=1, replica_groups=mesh['pb'=8,'kv'=32] {'kv'}, dimensions={0} | all-to-all | bytes 4194304 | tf_op jit(solution)/shard_map/all_to_all | solution.py:75
  422.7 2.3 copy.41
  (222 shorter events, 133.1 us)
Async XLA Ops:
  6.5 33.4 %all-gather.5.cloned.1.call-start = ((), (), s32[]{:S(2)}) async-start(), calls=%async_computation.5 | async-start | bytes 2359296 | tf_op jit(solution)/shard_map/all_gather | solution.py:25
  13.4 73.5 %all-to-all-start.1 = ((bf16[2,128,4096]{1,0,2:T(2,128)(2,1)}), bf16[2,128,4096]{1,0,2:T(2,128)(2,1)S(1)}, u32[]{:S(2)}, u32[]{:S(2)}) async-start(bf16[2,128,4096]{1,0,2:T(2,128)(2,1)} %copy.29), calls=%async_computation.1 | async-start | bytes 4194304 | tf_op jit(solution)/shard_map/all_to_all | solution.py:65
  86.9 59.9 %all-to-all-start.2 = ((bf16[32,256,128]{2,1,0:T(8,128)(2,1)}), bf16[32,256,128]{2,1,0:T(8,128)(2,1)}, u32[]{:S(2)}, u32[]{:S(2)}) async-start(bf16[32,256,128]{2,1,0:T(8,128)(2,1)} %constant_dynamic-update-slice_fusion.1), calls=%async_computation.2 | async-start | bytes 4194304 | tf_op jit(solution)/shard_map/all_to_all | solution.py:30
  97.1 30.4 %all-gather.3.cloned.1.call-start = ((), (), s32[]{:S(2)}) async-start(), calls=%async_computation.4 | async-start | bytes 2359296 | tf_op jit(solution)/shard_map/all_gather | solution.py:26
  146.8 6.5 %copy-start = (s32[64,8]{0,1:T(8,128)S(1)}, s32[64,8]{0,1:T(8,128)}, u32[]{:S(2)}) copy-start(s32[64,8]{0,1:T(8,128)} %param.10) | copy-start | bytes 6148
  146.8 6.6 %copy-start.1 = (s32[64]{0:T(128)S(1)}, s32[64]{0:T(128)}, u32[]{:S(2)}) copy-start(s32[64]{0:T(128)} %param.11) | copy-start | bytes 772
  146.8 55.8 %all-to-all-start = ((bf16[256,32,128]{0,2,1:T(8,128)(2,1)}), bf16[256,32,128]{0,2,1:T(8,128)(2,1)}, u32[]{:S(2)}, u32[]{:S(2)}) async-start(bf16[256,32,128]{0,2,1:T(8,128)(2,1)} %bitcast.202), calls=%async_computation | async-start | bytes 4194304 | tf_op jit(solution)/shard_map/all_to_all | solution.py:35
Sparse Core Ops, SparseCore 0:
  9.2 30.6 all-gather.4
  99.9 27.6 all-gather.2
